TPU v7x, 256 devices: a whole 4x4x8 slice. The times are simulated.
256 devices in a mesh: sample: 16 (over y, x_hi, core), filter: 16 (over x_lo, z).
Axes of the slice: x: 4 (x_hi: 2, x_lo: 2; x = x_hi * 2 + x_lo), y: 4, z: 8, core: 2. Of those that a mesh axis runs over, the one named last changes fastest.
Arguments:
- activations: bfloat16 [16, 2, 128, 2048], P('sample', None, None, 'filter'), may hold values from -18 to 18
- cotangent: bfloat16 [16, 2, 128, 2048], P('sample', None, None, 'filter'), may hold values from -2.5 to 2.5
- master_first: float32 [9, 2048, 2048], P(None, 'sample', 'filter'), may hold values from -0.046875 to 0.046875
- moment_first: float32 [9, 2048, 2048], P(None, 'sample', 'filter'), may hold values from -6 to 6
- second_first: float32 [9, 2048, 2048], P(None, 'sample', 'filter'), may hold values from 0.05 to 1
- master_second: float32 [9, 2048, 2048], P(None, 'sample', 'filter'), may hold values from -0.046875 to 0.046875
- moment_second: float32 [9, 2048, 2048], P(None, 'sample', 'filter'), may hold values from -6 to 6
- second_second: float32 [9, 2048, 2048], P(None, 'sample', 'filter'), may hold values from 0.05 to 1
Outputs:
- level_out: bfloat16 [16, 2, 128, 2048], P('sample', None, None, 'filter')
- input_grad: bfloat16 [16, 2, 128, 2048], P('sample', None, None, 'filter')
- new_master_first: float32 [9, 2048, 2048], P(None, 'sample', 'filter')
- new_moment_first: float32 [9, 2048, 2048], P(None, 'sample', 'filter')
- new_second_first: float32 [9, 2048, 2048], P(None, 'sample', 'filter')
- new_master_second: float32 [9, 2048, 2048], P(None, 'sample', 'filter')
- new_moment_second: float32 [9, 2048, 2048], P(None, 'sample', 'filter')
- new_second_second: float32 [9, 2048, 2048], P(None, 'sample', 'filter')
All inputs are finite; a program needn't handle non-finite values.
Results may differ from a plain program's by a relative error of at most 0.017.
Values may be sent and summed in bfloat16 or wider, within the bound.
No kernel may reach another device: no remote copies, remote signals or barrier semaphores. Data moves between devices by JAX's collectives and lax.ppermute only.
A program may use at most 128 MiB of HBM per device.

v0:
```python
import jax
import jax.numpy as jnp
from jax import lax
from jax.sharding import PartitionSpec as P

GROUP = 64
NORM_EPS = 1e-05
LEARN_RATE = 0.001
BETA_ONE = 0.9
BETA_TWO = 0.999
ADAM_EPS = 1e-08
CORRECT_ONE = 1.0 - 0.9**10
CORRECT_TWO = 1.0 - 0.999**10


def pad_slab(field):
    return jnp.pad(field, ((0, 0), (1, 1), (1, 1), (0, 0)))


def window(padded, row_start, column_start, height, breadth):
    return padded[:, row_start : row_start + height, column_start : column_start + breadth, :]


def conv_forward(source, weight):
    samples, height, breadth, depth_in = source.shape
    padded = pad_slab(source)
    summed = jnp.zeros((samples * height * breadth, weight.shape[2]), jnp.float32)
    for kernel_tap in range(9):
        shifted = window(padded, kernel_tap // 3, kernel_tap % 3, height, breadth)
        summed = summed + jnp.dot(
            shifted.reshape(samples * height * breadth, depth_in),
            weight[kernel_tap],
            preferred_element_type=jnp.float32,
        )
    return summed.reshape(samples, height, breadth, weight.shape[2])


def group_silu(pre_act):
    samples, height, breadth, depth_all = pre_act.shape
    grouped = pre_act.reshape(samples, height, breadth, depth_all // GROUP, GROUP)
    center = jnp.mean(grouped, axis=(1, 2, 4), keepdims=True)
    deviation = grouped - center
    spread = jnp.mean(deviation * deviation, axis=(1, 2, 4), keepdims=True)
    return jax.nn.silu(deviation * lax.rsqrt(spread + NORM_EPS)).reshape(pre_act.shape)


def tap_grads(source, upstream):
    samples, height, breadth, depth_in = source.shape
    padded = pad_slab(source)
    flat_up = upstream.reshape(samples, height * breadth, upstream.shape[3])
    results = []
    for kernel_tap in range(9):
        shifted = window(padded, kernel_tap // 3, kernel_tap % 3, height, breadth).reshape(
            samples, height * breadth, depth_in
        )
        results.append(
            lax.dot_general(
                shifted, flat_up, (((1,), (1,)), ((0,), (0,))), preferred_element_type=jnp.float32
            ).astype(jnp.bfloat16)
        )
    return jnp.stack(results, axis=1)


def adam_update(master, moment, second, gradient):
    moment_new = BETA_ONE * moment + (1.0 - BETA_ONE) * gradient
    second_new = BETA_TWO * second + (1.0 - BETA_TWO) * gradient * gradient
    step_size = moment_new / CORRECT_ONE / (jnp.sqrt(second_new / CORRECT_TWO) + ADAM_EPS)
    return (master - LEARN_RATE * step_size, moment_new, second_new)


def full_weight(master):
    return lax.all_gather(master.astype(jnp.bfloat16), "sample", axis=1, tiled=True)


def keep_panels(source):
    return lax.all_gather(source, "filter", axis=3, tiled=True)


def data_grad(upstream, weight):
    samples, height, breadth, depth_out = upstream.shape
    cell_count = samples * height * breadth
    padded = pad_slab(upstream)
    shifted_all = [
        window(padded, 2 - kernel_tap // 3, 2 - kernel_tap % 3, height, breadth).reshape(
            cell_count, depth_out
        )
        for kernel_tap in range(9)
    ]
    local_rows = weight.shape[1] // lax.axis_size("filter")
    summed = jnp.zeros((local_rows * lax.axis_size("filter"), cell_count), jnp.float32)
    for kernel_tap in range(9):
        summed = summed + lax.dot_general(
            weight[kernel_tap],
            shifted_all[kernel_tap],
            (((1,), (1,)), ((), ())),
            preferred_element_type=jnp.float32,
        )
    own_rows = lax.psum_scatter(
        summed.astype(jnp.bfloat16), "filter", scatter_dimension=0, tiled=True
    ).astype(jnp.float32)
    return own_rows.T.reshape(samples, height, breadth, local_rows)


def filter_grad(whole, upstream):
    partial_sum = tap_grads(whole, upstream)[0].astype(jnp.float32)
    return lax.psum_scatter(
        partial_sum.astype(jnp.bfloat16), "sample", scatter_dimension=1, tiled=True
    ).astype(jnp.float32)


def per_device(
    activations,
    cotangent,
    master_first,
    moment_first,
    second_first,
    master_second,
    moment_second,
    second_second,
):
    weight_first = full_weight(master_first)
    weight_second = full_weight(master_second)
    whole_input = keep_panels(activations)
    pre_first = conv_forward(whole_input, weight_first)
    hidden = group_silu(pre_first).astype(jnp.bfloat16)
    whole_hidden = keep_panels(hidden)
    pre_second = conv_forward(whole_hidden, weight_second)
    level_out = (activations.astype(jnp.float32) + pre_second).astype(jnp.bfloat16)
    hidden_grad = data_grad(cotangent, weight_second)
    _, pullback = jax.vjp(group_silu, pre_first)
    pre_grad = pullback(hidden_grad)[0].astype(jnp.bfloat16)
    input_grad = (cotangent.astype(jnp.float32) + data_grad(pre_grad, weight_first)).astype(
        jnp.bfloat16
    )
    grad_second = filter_grad(whole_hidden, cotangent)
    grad_first = filter_grad(whole_input, pre_grad)
    new_master_first, new_moment_first, new_second_first = adam_update(
        master_first, moment_first, second_first, grad_first
    )
    new_master_second, new_moment_second, new_second_second = adam_update(
        master_second, moment_second, second_second, grad_second
    )
    return (
        level_out,
        input_grad,
        new_master_first,
        new_moment_first,
        new_second_first,
        new_master_second,
        new_moment_second,
        new_second_second,
    )


def solution(mesh):
    placed = (
        P("sample", None, None, "filter"),
        P("sample", None, None, "filter"),
        P(None, "sample", "filter"),
        P(None, "sample", "filter"),
        P(None, "sample", "filter"),
        P(None, "sample", "filter"),
        P(None, "sample", "filter"),
        P(None, "sample", "filter"),
    )
    return jax.shard_map(
        per_device,
        mesh=mesh,
        in_specs=placed,
        out_specs=(
            P("sample", None, None, "filter"),
            P("sample", None, None, "filter"),
            P(None, "sample", "filter"),
            P(None, "sample", "filter"),
            P(None, "sample", "filter"),
            P(None, "sample", "filter"),
            P(None, "sample", "filter"),
            P(None, "sample", "filter"),
        ),
        check_vma=False,
    )
```

profile of v0, /device:TPU:32, one launch (start us, length us, event | category | flops | bytes accessed | tf_op | source)
XLA Modules:
  0.0 662.6 jit_solution(3601517996749550026)
XLA Ops:
  7.9 1.8 convert_element_type.155
  9.8 66.3 %all-gather.5.cloned.1.call-done = bf16[1,2,128,2048]{3,2,1,0:T(8,128)(2,1)} async-done(((bf16[1,2,128,128]{3,2,1,0:T(8,128)(2,1)}), bf16[1,2,128,2048]{3,2,1,0:T(8,128)(2,1)}) %all-gather.5.cloned.1.call-update) | async-done | bytes 1048592 | tf_op jit(solution)/shard_map/all_gather | solution.py:76
  76.1 5.0 pad_slice_fusion.8
  81.1 60.8 %all-gather.7.cloned.1.call-done = bf16[9,2048,128]{2,1,0:T(8,128)(2,1)} async-done(((bf16[9,128,128]{2,1,0:T(8,128)(2,1)}), bf16[9,2048,128]{2,1,0:T(8,128)(2,1)}) %all-gather.7.cloned.1.call-update) | async-done | bytes 4718608 | tf_op jit(solution)/shard_map/all_gather | solution.py:72
  141.9 1.9 fusion.67
  143.9 2.3 convolution_add_fusion.27
  146.2 1.8 convolution_add_fusion.26
  148.0 1.7 convolution_add_fusion.25
  153.6 66.1 %all-gather.9.cloned.1.call-done = bf16[1,2,128,2048]{2,3,1,0:T(8,128)(2,1)} async-done(((bf16[1,2,128,128]{2,3,1,0:T(8,128)(2,1)}), bf16[1,2,128,2048]{2,3,1,0:T(8,128)(2,1)}) %all-gather.9.cloned.1.call-update) | async-done | bytes 1048592 | tf_op jit(solution)/shard_map/all_gather | solution.py:76
  219.8 1.6 fusion.52
  221.4 1.6 fusion.50
  223.0 1.6 fusion.48
  228.2 2.1 copy-done.9
  230.4 88.9 %reduce-scatter.11.cloned.1.call-done = bf16[9,128,128]{2,1,0:T(8,128)(2,1)} async-done(((bf16[9,2048,128]{2,1,0:T(8,128)(2,1)}), bf16[9,128,128]{2,1,0:T(8,128)(2,1)}) %reduce-scatter.11.cloned.1.call-update) | async-done | bytes 294928 | tf_op jit(solution)/shard_map/reduce_scatter | solution.py:106
  319.3 3.3 multiply_subtract_fusion
  323.7 59.9 %all-gather.11.cloned.1.call-done = bf16[9,2048,128]{2,1,0:T(8,128)(2,1)} async-done(((bf16[9,128,128]{2,1,0:T(8,128)(2,1)}), bf16[9,2048,128]{2,1,0:T(8,128)(2,1)}) %all-gather.11.cloned.1.call-update) | async-done | bytes 4718608 | tf_op jit(solution)/shard_map/all_gather | solution.py:72
  383.6 1.7 fusion.68
  385.3 1.5 convolution_bitcast_fusion.1
  389.5 1.6 fusion.6
  391.1 2.3 copy.67
  393.5 68.0 %reduce-scatter.13.cloned.1.call-done = bf16[128,256]{1,0:T(8,128)(2,1)} async-done(((bf16[2048,256]{1,0:T(8,128)(2,1)}), bf16[128,256]{1,0:T(8,128)(2,1)}) %reduce-scatter.13.cloned.1.call-update) | async-done | bytes 65552
  466.3 2.5 fusion.18
  468.8 1.7 copy.54
  472.3 1.6 copy.56
  473.9 1.6 copy.57
  475.5 1.6 copy.58
  480.0 1.7 fusion.66
  481.7 1.6 convolution_add_fusion.7
  483.3 1.5 convolution_add_fusion.6
  488.5 2.3 copy.69
  491.0 2.7 fusion.20
  493.7 2.5 fusion.22
  496.3 2.5 fusion.24
  505.4 3.6 pad_slice_fusion
  509.0 2.3 copy.44
  511.3 2.3 copy.45
  513.5 2.3 copy.46
  515.8 2.3 copy.47
  518.1 2.3 copy.49
  520.4 2.3 copy.50
  525.9 1.9 fusion.69
  527.8 1.9 convolution_add_fusion.19
  529.7 1.9 convolution_add_fusion.18
  533.1 1.5 convolution_add_fusion.16
  534.6 1.5 convolution_add_fusion.15
  540.5 18.8 %reduce-scatter.15.cloned.1.call-done = bf16[128,256]{1,0:T(8,128)(2,1)} async-done(((bf16[2048,256]{1,0:T(8,128)(2,1)}), bf16[128,256]{1,0:T(8,128)(2,1)}) %reduce-scatter.15.cloned.1.call-update) | async-done | bytes 65552
  561.0 91.8 %reduce-scatter.9.cloned.1.call-done = bf16[9,128,128]{2,1,0:T(8,128)(2,1)} async-done(((bf16[9,2048,128]{2,1,0:T(8,128)(2,1)}), bf16[9,128,128]{2,1,0:T(8,128)(2,1)}) %reduce-scatter.9.cloned.1.call-update) | async-done | bytes 294928 | tf_op jit(solution)/shard_map/reduce_scatter | solution.py:106
  652.7 3.0 multiply_subtract_fusion.1
  (144 shorter events, 42.9 us)
Async XLA Ops:
  7.2 69.0 %all-gather.5.cloned.1.call-start = ((), (), s32[]{:S(2)}) async-start(), calls=%async_computation.4 | async-start | bytes 1114112 | tf_op jit(solution)/shard_map/all_gather | solution.py:76
  7.9 134.0 %all-gather.7.cloned.1.call-start = ((), (), s32[]{:S(2)}) async-start(), calls=%async_computation.5 | async-start | bytes 5013504 | tf_op jit(solution)/shard_map/all_gather | solution.py:72
  9.8 209.9 %all-gather.9.cloned.1.call-start = ((), (), s32[]{:S(2)}) async-start(), calls=%async_computation.6 | async-start | bytes 1114112 | tf_op jit(solution)/shard_map/all_gather | solution.py:76
  141.9 6.1 copy-start.1
  141.9 7.8 %copy-start.2 = (bf16[1,2,128,2048]{3,2,1,0:T(8,128)(2,1)S(1)}, bf16[1,2,128,2048]{3,2,1,0:T(8,128)(2,1)}, u32[]{:S(2)}) copy-start(bf16[1,2,128,2048]{3,2,1,0:T(8,128)(2,1)} %all-gather.5.cloned.1.call-done) | copy-start | bytes 3145732
  141.9 8.2 %copy-start.5 = (bf16[1,2,128,2048]{3,2,1,0:T(8,128)(2,1)S(1)}, bf16[1,2,128,2048]{3,2,1,0:T(8,128)(2,1)}, u32[]{:S(2)}) copy-start(bf16[1,2,128,2048]{3,2,1,0:T(8,128)(2,1)} %get-tuple-element.28) | copy-start | bytes 3145732
  143.9 6.7 %copy-start.3 = (bf16[1,2,128,2048]{3,2,1,0:T(8,128)(2,1)S(1)}, bf16[1,2,128,2048]{3,2,1,0:T(8,128)(2,1)}, u32[]{:S(2)}) copy-start(bf16[1,2,128,2048]{3,2,1,0:T(8,128)(2,1)} %get-tuple-element.29) | copy-start | bytes 3145732
  149.7 70.1 %copy-start.15 = (bf16[1,2,128,128]{3,2,1,0:T(8,128)(2,1)S(1)}, bf16[1,2,128,128]{3,2,1,0:T(8,128)(2,1)}, u32[]{:S(2)}) copy-start(bf16[1,2,128,128]{3,2,1,0:T(8,128)(2,1)} %param.9) | copy-start | bytes 196612
  152.5 73.3 %copy-start.24 = (f32[2]{0:T(128)}, f32[2]{0:T(128)S(1)}, u32[]{:S(2)}) copy-start(f32[2]{0:T(128)S(1)} %reduce_sum.85) | copy-start | bytes 28
  153.6 165.8 %reduce-scatter.11.cloned.1.call-start = ((), (), s32[]{:S(2)}) async-start(), calls=%async_computation.9 | async-start | bytes 5013504 | tf_op jit(solution)/shard_map/reduce_scatter | solution.py:106
  219.8 4.8 copy-start.7
  228.2 2.1 copy-start.9
  230.4 153.2 %all-gather.11.cloned.1.call-start = ((), (), s32[]{:S(2)}) async-start(), calls=%async_computation.7 | async-start | bytes 5013504 | tf_op jit(solution)/shard_map/all_gather | solution.py:72
  322.6 138.9 %reduce-scatter.13.cloned.1.call-start = ((), (), s32[]{:S(2)}) async-start(), calls=%async_computation.10 | async-start | bytes 1114112
  383.6 3.2 copy-start
  383.6 3.2 copy-start.23
  383.6 3.6 copy-start.22
  383.6 4.1 copy-start.18
  386.8 1.4 copy-start.17
  387.7 0.9 copy-start.16
  393.4 165.9 %reduce-scatter.15.cloned.1.call-start = ((), (), s32[]{:S(2)}) async-start(), calls=%async_computation.11 | async-start | bytes 1114112
  480.0 3.3 copy-start.20
  480.0 4.8 slice-start
  481.7 3.1 slice-start.1
  481.7 3.1 copy-start.19
  490.8 162.0 %reduce-scatter.9.cloned.1.call-start = ((), (), s32[]{:S(2)}) async-start(), calls=%async_computation.8 | async-start | bytes 5013504 | tf_op jit(solution)/shard_map/reduce_scatter | solution.py:106
  491.0 9.1 %copy-start.6 = (bf16[1,2,128,2048]{3,2,1,0:T(8,128)(2,1)S(1)}, bf16[1,2,128,2048]{3,2,1,0:T(8,128)(2,1)}, u32[]{:S(2)}) copy-start(bf16[1,2,128,2048]{3,2,1,0:T(8,128)(2,1)} %get-tuple-element.28) | copy-start | bytes 3145732
  491.0 10.4 %copy-start.4 = (bf16[1,2,128,2048]{3,2,1,0:T(8,128)(2,1)S(1)}, bf16[1,2,128,2048]{3,2,1,0:T(8,128)(2,1)}, u32[]{:S(2)}) copy-start(bf16[1,2,128,2048]{3,2,1,0:T(8,128)(2,1)} %get-tuple-element.29) | copy-start | bytes 3145732
  501.4 3.9 copy-start.8
  525.9 5.7 copy-start.13
  525.9 7.2 %copy-start.14 = (bf16[1,2,128,2048]{3,2,1,0:T(8,128)(2,1)S(1)}, bf16[1,2,128,2048]{3,2,1,0:T(8,128)(2,1)}, u32[]{:S(2)}) copy-start(bf16[1,2,128,2048]{3,2,1,0:T(8,128)(2,1)} %copy.48) | copy-start | bytes 3145732
  525.9 8.7 %copy-start.12 = (bf16[1,2,128,2048]{3,2,1,0:T(8,128)(2,1)S(1)}, bf16[1,2,128,2048]{3,2,1,0:T(8,128)(2,1)}, u32[]{:S(2)}) copy-start(bf16[1,2,128,2048]{3,2,1,0:T(8,128)(2,1)} %copy.49) | copy-start | bytes 3145732
  527.8 8.3 %copy-start.11 = (bf16[1,2,128,2048]{3,2,1,0:T(8,128)(2,1)S(1)}, bf16[1,2,128,2048]{3,2,1,0:T(8,128)(2,1)}, u32[]{:S(2)}) copy-start(bf16[1,2,128,2048]{3,2,1,0:T(8,128)(2,1)} %copy.50) | copy-start | bytes 3145732
  529.7 7.9 %copy-start.10 = (bf16[1,2,128,2048]{3,2,1,0:T(8,128)(2,1)S(1)}, bf16[1,2,128,2048]{3,2,1,0:T(8,128)(2,1)}, u32[]{:S(2)}) copy-start(bf16[1,2,128,2048]{3,2,1,0:T(8,128)(2,1)} %copy.51) | copy-start | bytes 3145732
  533.1 27.2 %copy-start.21 = (bf16[1,2,128,128]{3,2,1,0:T(8,128)(2,1)S(1)}, bf16[1,2,128,128]{3,2,1,0:T(8,128)(2,1)}, u32[]{:S(2)}) copy-start(bf16[1,2,128,128]{3,2,1,0:T(8,128)(2,1)} %param.8) | copy-start | bytes 196612
Sparse Core Ops, SparseCore 0:
  9.7 66.3 all-gather.4
  79.4 62.4 all-gather.6
  153.7 65.9 all-gather.8
  230.5 88.8 reduce-scatter.10
  322.7 60.7 all-gather.10
  393.6 67.8 reduce-scatter.12
  490.9 68.3 reduce-scatter.14
  563.7 88.9 reduce-scatter.8
where the time goes:
time: 664 us; the launch traced here: 663 us
  waiting for transfers between devices  521 us (78%)
  matrix products  65.3 us (10%)
  local copies, waits for them, and re-layouts  46.1 us (7%)
  between operations  14.8 us (2%)
  other arithmetic  14.2 us (2%)
    reduce_scatter x2, waiting for transfers between devices, filter_grad(): lax.psum_scatter(partial_sum.astype(jnp.bfloat16), 'sample', scatter_dime...  181 us
    all_gather x2, waiting for transfers between devices, keep_panels(): return lax.all_gather(source, 'filter', axis=3, tiled=True)  132 us
    all_gather x2, waiting for transfers between devices, full_weight(): lax.all_gather(master.astype(jnp.bfloat16), 'sample', axis=1, tiled=True)  121 us
    unnamed x10, waiting for transfers between devices  87.6 us
    slice x20, local copies, waits for them, and re-layouts, window(): padded[:, row_start:row_start + height, column_start:column_start + bread...  33.4 us
    dot_general x18, matrix products, tap_grads(): lax.dot_general(shifted, flat_up, (((1,), (1,)), ((0,), (0,))), preferred...  25.2 us
    dot_general x18, matrix products, conv_forward(): jnp.dot(shifted.reshape(samples * height * breadth, depth_in), weight[ker...  24.4 us
    dot_general x18, matrix products, data_grad(): lax.dot_general(weight[kernel_tap], shifted_all[kernel_tap], (((1,), (1,)...  15.7 us
  transfers between devices with their start and end apart: 8, of which 8 were waited for; matrix products, arithmetic and copies ran while one was open for 9% of the time, Pallas kernels for 0%

commit v1 on v0

--- a/solution.py
+++ b/solution.py
@@ -73,7 +73,14 @@
 
 
 def keep_panels(source):
-    return lax.all_gather(source, "filter", axis=3, tiled=True)
+
+    def wait_matrix(axis_id, vals):
+        far_arr = lax.psum(1, axis_id)
+        piece_next = jnp.stack([vals] * far_arr)
+        local_part = lax.all_to_all(piece_next, axis_name=axis_id, split_axis=0, concat_axis=0)
+        return jnp.concatenate(local_part, axis=3)
+
+    return wait_matrix("filter", source)
 
 
 def data_grad(upstream, weight):

time: 664 us -> 562 us (0.85)
  waiting for transfers between devices: 521 us -> 341 us
  blocking collectives: 0 us -> 69.8 us
    all_gather x2 -> x0, waiting for transfers between devices: 132 us -> none  [keep_panels(): return lax.all_gather(source, 'filter', axis=3, tiled=True)]
    all_to_all x0 -> x2, blocking collectives: none -> 69.8 us  [wait_matrix(): lax.all_to_all(piece_next, axis_name=axis_id, split_axis=0, concat_axis=0)]
    all_gather x2, waiting for transfers between devices: 121 us -> 73.8 us  [full_weight(): lax.all_gather(master.astype(jnp.bfloat16), 'sample', axis=1, tiled=True)]
    unnamed x10 -> x8, waiting for transfers between devices: 87.6 us -> 89.4 us
  transfers between devices with their start and end apart: 8 -> 6, of which waited for: 8 -> 6; matrix products, arithmetic and copies ran while one was open for 9% -> 12% of each run, Pallas kernels for 0% -> 0%
where the time goes in v1:
time: 562 us; the launch traced here: 561 us
  waiting for transfers between devices  341 us (61%)
  matrix products  71.3 us (13%)
  blocking collectives  69.8 us (12%)
  local copies, waits for them, and re-layouts  51.5 us (9%)
  between operations  14.7 us (3%)
  other arithmetic  11.8 us (2%)
    reduce_scatter x2, waiting for transfers between devices, filter_grad(): lax.psum_scatter(partial_sum.astype(jnp.bfloat16), 'sample', scatter_dime...  178 us
    unnamed x8, waiting for transfers between devices  89.4 us
    all_gather x2, waiting for transfers between devices, full_weight(): lax.all_gather(master.astype(jnp.bfloat16), 'sample', axis=1, tiled=True)  73.8 us
    all_to_all x2, blocking collectives, wait_matrix(): lax.all_to_all(piece_next, axis_name=axis_id, split_axis=0, concat_axis=0)  69.8 us
    slice x20, local copies, waits for them, and re-layouts, window(): padded[:, row_start:row_start + height, column_start:column_start + bread...  35.8 us
    dot_general x18, matrix products, tap_grads(): lax.dot_general(shifted, flat_up, (((1,), (1,)), ((0,), (0,))), preferred...  31.8 us
    dot_general x18, matrix products, conv_forward(): jnp.dot(shifted.reshape(samples * height * breadth, depth_in), weight[ker...  23.9 us
    dot_general x18, matrix products, data_grad(): lax.dot_general(weight[kernel_tap], shifted_all[kernel_tap], (((1,), (1,)...  15.6 us
  transfers between devices with their start and end apart: 6, of which 6 were waited for; matrix products, arithmetic and copies ran while one was open for 12% of the time, Pallas kernels for 0%

profile of v1, /device:TPU:32, one launch (start us, length us, event | category | flops | bytes accessed | tf_op | source)
XLA Modules:
  0.0 561.0 jit_solution(617416613159496535)
XLA Ops:
  7.2 1.8 convert_element_type.154
  10.3 35.5 %all_to_all.10 = bf16[16,1,2,128,128]{3,4,2,1,0:T(8,128)(2,1)S(1)} all-to-all(bf16[16,1,2,128,128]{3,4,2,1,0:T(8,128)(2,1)S(1)} %stack.44), channel_id=1, replica_groups=mesh['sample'=16,'filter'=16] {'filter'}, dimensions={0} | all-to-all | bytes 2097152 | tf_op jit(solution)/shard_map/all_to_all | solution.py:80
  45.9 1.7 copy.59
  47.6 3.7 pad_slice_fusion.8
  51.3 2.4 copy.63
  53.7 2.3 copy.56
  56.0 2.3 copy.57
  62.1 2.3 copy.55
  64.4 13.7 %all-gather.3.cloned.1.call-done = bf16[9,2048,128]{2,1,0:T(8,128)(2,1)} async-done(((bf16[9,128,128]{2,1,0:T(8,128)(2,1)}), bf16[9,2048,128]{2,1,0:T(8,128)(2,1)}) %all-gather.3.cloned.1.call-update) | async-done | bytes 4718608 | tf_op jit(solution)/shard_map/all_gather | solution.py:72
  78.1 1.9 fusion.73
  80.1 2.0 convolution_add_fusion.27
  82.1 1.8 convolution_add_fusion.26
  83.9 1.7 convolution_add_fusion.25
  89.0 34.3 %all_to_all.11 = bf16[16,1,2,128,128]{4,3,2,1,0:T(8,128)(2,1)S(1)} all-to-all(bf16[16,1,2,128,128]{4,3,2,1,0:T(8,128)(2,1)S(1)} %stack.45), channel_id=1, replica_groups=mesh['sample'=16,'filter'=16] {'filter'}, dimensions={0} | all-to-all | bytes 2097152 | tf_op jit(solution)/shard_map/all_to_all | solution.py:80
  124.2 1.6 copy.69
  125.9 2.3 copy.64
  128.2 2.5 fusion.51
  130.7 2.3 fusion.49
  132.9 2.3 fusion.47
  143.2 86.4 %reduce-scatter.11.cloned.1.call-done = bf16[9,128,128]{2,1,0:T(8,128)(2,1)} async-done(((bf16[9,2048,128]{2,1,0:T(8,128)(2,1)}), bf16[9,128,128]{2,1,0:T(8,128)(2,1)}) %reduce-scatter.11.cloned.1.call-update) | async-done | bytes 294928 | tf_op jit(solution)/shard_map/reduce_scatter | solution.py:113
  229.7 3.3 multiply_subtract_fusion
  233.7 60.1 %all-gather.5.cloned.1.call-done = bf16[9,2048,128]{2,1,0:T(8,128)(2,1)} async-done(((bf16[9,128,128]{2,1,0:T(8,128)(2,1)}), bf16[9,2048,128]{2,1,0:T(8,128)(2,1)}) %all-gather.5.cloned.1.call-update) | async-done | bytes 4718608 | tf_op jit(solution)/shard_map/all_gather | solution.py:72
  293.9 1.7 convolution_bitcast_fusion
  295.5 1.5 convolution_bitcast_fusion.1
  299.8 1.6 fusion.6
  301.3 2.3 copy.78
  303.7 68.1 %reduce-scatter.13.cloned.1.call-done = bf16[128,256]{1,0:T(8,128)(2,1)} async-done(((bf16[2048,256]{1,0:T(8,128)(2,1)}), bf16[128,256]{1,0:T(8,128)(2,1)}) %reduce-scatter.13.cloned.1.call-update) | async-done | bytes 65552
  376.0 2.5 fusion.17
  378.6 1.6 fusion.72
  380.2 1.5 convolution_add_fusion.7
  386.9 2.3 copy.80
  389.5 2.6 fusion.19
  392.1 2.6 fusion.21
  394.7 2.5 fusion.23
  403.9 3.6 pad_slice_fusion
  407.5 2.3 copy.73
  409.8 2.4 copy.66
  412.1 2.3 copy.67
  414.4 2.3 copy.68
  416.7 2.3 copy.70
  422.2 1.6 fusion.75
  423.8 1.9 convolution_add_fusion.19
  425.7 1.6 convolution_add_fusion.18
  427.3 1.9 convolution_add_fusion.17
  429.2 1.5 convolution_add_fusion.16
  436.6 21.2 %reduce-scatter.15.cloned.1.call-done = bf16[128,256]{1,0:T(8,128)(2,1)} async-done(((bf16[2048,256]{1,0:T(8,128)(2,1)}), bf16[128,256]{1,0:T(8,128)(2,1)}) %reduce-scatter.15.cloned.1.call-update) | async-done | bytes 65552
  459.5 91.7 %reduce-scatter.9.cloned.1.call-done = bf16[9,128,128]{2,1,0:T(8,128)(2,1)} async-done(((bf16[9,2048,128]{2,1,0:T(8,128)(2,1)}), bf16[9,128,128]{2,1,0:T(8,128)(2,1)}) %reduce-scatter.9.cloned.1.call-update) | async-done | bytes 294928 | tf_op jit(solution)/shard_map/reduce_scatter | solution.py:113
  551.2 3.0 multiply_subtract_fusion.1
  (142 shorter events, 47.9 us)
Async XLA Ops:
  7.2 71.0 %all-gather.3.cloned.1.call-start = ((), (), s32[]{:S(2)}) async-start(), calls=%async_computation.6 | async-start | bytes 5013504 | tf_op jit(solution)/shard_map/all_gather | solution.py:72
  9.1 220.6 %reduce-scatter.11.cloned.1.call-start = ((), (), s32[]{:S(2)}) async-start(), calls=%async_computation.9 | async-start | bytes 5013504 | tf_op jit(solution)/shard_map/reduce_scatter | solution.py:113
  51.3 6.9 %copy-start.8 = (bf16[1,2,128,2048]{2,3,1,0:T(8,128)(2,1)S(1)}, bf16[1,2,128,2048]{2,3,1,0:T(8,128)(2,1)}, u32[]{:S(2)}) copy-start(bf16[1,2,128,2048]{2,3,1,0:T(8,128)(2,1)} %get-tuple-element.27) | copy-start | bytes 3145732
  78.1 5.8 %copy-start.1 = (bf16[9,2048,128]{2,1,0:T(8,128)(2,1)S(1)}, bf16[9,2048,128]{2,1,0:T(8,128)(2,1)}, u32[]{:S(2)}) copy-start(bf16[9,2048,128]{2,1,0:T(8,128)(2,1)} %all-gather.3.cloned.1.call-done) | copy-start | bytes 14155780
  78.1 7.5 %copy-start.14 = (bf16[1,2,128,16,128]{4,3,2,1,0:T(8,128)(2,1)S(1)}, bf16[1,2,128,16,128]{4,3,2,1,0:T(8,128)(2,1)}, u32[]{:S(2)}) copy-start(bf16[1,2,128,16,128]{4,3,2,1,0:T(8,128)(2,1)} %copy.59) | copy-start | bytes 3145732
  83.9 3.5 copy-start.2
  87.4 40.8 %copy-start.18 = (bf16[1,2,128,128]{3,2,1,0:T(8,128)(2,1)S(1)}, bf16[1,2,128,128]{3,2,1,0:T(8,128)(2,1)}, u32[]{:S(2)}) copy-start(bf16[1,2,128,128]{3,2,1,0:T(8,128)(2,1)} %param.9) | copy-start | bytes 196612
  88.5 42.2 %copy-start.23 = (f32[2]{0:T(128)}, f32[2]{0:T(128)S(1)}, u32[]{:S(2)}) copy-start(f32[2]{0:T(128)S(1)} %reduce_sum.85) | copy-start | bytes 28
  123.3 1.0 copy-start.4
  128.2 7.1 %copy-start.5 = (bf16[1,2,128,16,128]{2,4,3,1,0:T(8,128)(2,1)S(1)}, bf16[1,2,128,16,128]{2,4,3,1,0:T(8,128)(2,1)}, u32[]{:S(2)}) copy-start(bf16[1,2,128,16,128]{2,4,3,1,0:T(8,128)(2,1)} %copy.64) | copy-start | bytes 3145732
  128.2 8.5 %copy-start.16 = (bf16[1,2,128,16,128]{4,3,2,1,0:T(8,128)(2,1)S(1)}, bf16[1,2,128,16,128]{4,3,2,1,0:T(8,128)(2,1)}, u32[]{:S(2)}) copy-start(bf16[1,2,128,16,128]{4,3,2,1,0:T(8,128)(2,1)} %copy.69) | copy-start | bytes 3145732
  143.2 150.7 %all-gather.5.cloned.1.call-start = ((), (), s32[]{:S(2)}) async-start(), calls=%async_computation.7 | async-start | bytes 5013504 | tf_op jit(solution)/shard_map/all_gather | solution.py:72
  232.9 138.8 %reduce-scatter.13.cloned.1.call-start = ((), (), s32[]{:S(2)}) async-start(), calls=%async_computation.10 | async-start | bytes 1114112
  293.9 3.2 copy-start
  293.9 3.2 copy-start.22
  293.9 3.6 copy-start.21
  293.9 4.1 copy-start.19
  303.6 154.2 %reduce-scatter.15.cloned.1.call-start = ((), (), s32[]{:S(2)}) async-start(), calls=%async_computation.11 | async-start | bytes 1114112
  378.6 4.7 slice-start
  380.2 3.1 slice-start.1
  389.2 162.0 %reduce-scatter.9.cloned.1.call-start = ((), (), s32[]{:S(2)}) async-start(), calls=%async_computation.8 | async-start | bytes 5013504 | tf_op jit(solution)/shard_map/reduce_scatter | solution.py:113
  389.5 7.7 %copy-start.15 = (bf16[1,2,128,16,128]{4,3,2,1,0:T(8,128)(2,1)S(1)}, bf16[1,2,128,16,128]{4,3,2,1,0:T(8,128)(2,1)}, u32[]{:S(2)}) copy-start(bf16[1,2,128,16,128]{4,3,2,1,0:T(8,128)(2,1)} %copy.59) | copy-start | bytes 3145732
  392.1 10.4 %copy-start.3 = (bf16[1,2,128,2048]{3,2,1,0:T(8,128)(2,1)S(1)}, bf16[1,2,128,2048]{3,2,1,0:T(8,128)(2,1)}, u32[]{:S(2)}) copy-start(bf16[1,2,128,2048]{3,2,1,0:T(8,128)(2,1)} %copy.63) | copy-start | bytes 3145732
  399.9 4.0 copy-start.6
  409.8 9.2 %copy-start.7 = (bf16[1,2,128,2048]{2,3,1,0:T(8,128)(2,1)S(1)}, bf16[1,2,128,2048]{2,3,1,0:T(8,128)(2,1)}, u32[]{:S(2)}) copy-start(bf16[1,2,128,2048]{2,3,1,0:T(8,128)(2,1)} %get-tuple-element.21) | copy-start | bytes 3145732
  420.3 5.4 copy-start.13
  422.1 7.0 %copy-start.17 = (bf16[1,2,128,16,128]{4,3,2,1,0:T(8,128)(2,1)S(1)}, bf16[1,2,128,16,128]{4,3,2,1,0:T(8,128)(2,1)}, u32[]{:S(2)}) copy-start(bf16[1,2,128,16,128]{4,3,2,1,0:T(8,128)(2,1)} %copy.69) | copy-start | bytes 3145732
  422.2 8.5 %copy-start.12 = (bf16[1,2,128,2048]{3,2,1,0:T(8,128)(2,1)S(1)}, bf16[1,2,128,2048]{3,2,1,0:T(8,128)(2,1)}, u32[]{:S(2)}) copy-start(bf16[1,2,128,2048]{3,2,1,0:T(8,128)(2,1)} %copy.70) | copy-start | bytes 3145732
  423.8 8.4 %copy-start.11 = (bf16[1,2,128,2048]{3,2,1,0:T(8,128)(2,1)S(1)}, bf16[1,2,128,2048]{3,2,1,0:T(8,128)(2,1)}, u32[]{:S(2)}) copy-start(bf16[1,2,128,2048]{3,2,1,0:T(8,128)(2,1)} %copy.71) | copy-start | bytes 3145732
  425.7 8.0 %copy-start.10 = (bf16[1,2,128,2048]{3,2,1,0:T(8,128)(2,1)S(1)}, bf16[1,2,128,2048]{3,2,1,0:T(8,128)(2,1)}, u32[]{:S(2)}) copy-start(bf16[1,2,128,2048]{3,2,1,0:T(8,128)(2,1)} %copy.72) | copy-start | bytes 3145732
  427.3 7.9 %copy-start.9 = (bf16[1,2,128,2048]{3,2,1,0:T(8,128)(2,1)S(1)}, bf16[1,2,128,2048]{3,2,1,0:T(8,128)(2,1)}, u32[]{:S(2)}) copy-start(bf16[1,2,128,2048]{3,2,1,0:T(8,128)(2,1)} %copy.73) | copy-start | bytes 3145732
  429.2 29.7 %copy-start.20 = (bf16[1,2,128,128]{3,2,1,0:T(8,128)(2,1)S(1)}, bf16[1,2,128,128]{3,2,1,0:T(8,128)(2,1)}, u32[]{:S(2)}) copy-start(bf16[1,2,128,128]{3,2,1,0:T(8,128)(2,1)} %param.8) | copy-start | bytes 196612
Sparse Core Ops, SparseCore 0:
  11.3 66.7 all-gather.2
  143.3 86.3 reduce-scatter.10
  233.1 60.7 all-gather.4
  303.8 67.9 reduce-scatter.12
  389.4 68.4 reduce-scatter.14
  462.1 89.0 reduce-scatter.8
